TPU v7x, 256 devices: a whole 4x4x8 slice. The times are simulated.
256 devices in a mesh: pipe: 2 (over core), seq: 4 (over x), tensor: 32 (over z, y).
Axes of the slice: x: 4, y: 4, z: 8, core: 2. Of those that a mesh axis runs over, the one named last changes fastest.
Arguments:
- token_ids: int32 [2, 768], P(None, 'seq'), may hold values from 0 to 511
- embed_table: bfloat16 [512, 8192], P(None, 'tensor'), may hold values from -24 to 24
- in_proj: bfloat16 [2, 8192, 3, 4096], P('pipe', None, None, 'tensor'), may hold values from -0.0625 to 0.0625
- feat_taps: float32 [2, 3, 3, 4096], P('pipe', None, None, 'tensor'), may hold values from -3 to 3
- se_taps: float32 [7, 4096], P(None, 'tensor'), may hold values from -2 to 2
- mr_taps: float32 [128, 4096], P(None, 'tensor'), may hold values from -0.6 to 0.6
- out_proj: bfloat16 [2, 4096, 8192], P('pipe', 'tensor'), may hold values from -0.1875 to 0.1875
- norm_gain: bfloat16 [2, 8192], P('pipe', 'tensor'), may hold values from 0.25 to 1.75
Outputs:
- segment_out: bfloat16 [2, 2, 768, 8192], P('pipe', None, 'seq', 'tensor')
All inputs are finite; a program needn't handle non-finite values.
Results may differ from a plain program's by a relative error of at most 0.023.
Values may be sent and summed in bfloat16 or wider, within the bound.
No kernel may reach another device: no remote copies, remote signals or barrier semaphores. Data moves between devices by JAX's collectives and lax.ppermute only.
A program may use at most 64 MiB of HBM per device.

v0:
```python
import jax
import jax.numpy as jnp
from jax import lax
from jax.sharding import PartitionSpec as P

VOCAB = 512
KL = 128
KS = 7
KF = 3
HALO = KL + KF - 2
epsilon = 1e-06


def swapped(value):
    return lax.ppermute(value, "pipe", [(0, 1), (1, 0)])


def of_section(core, own, other, section):
    return jnp.where(core == section, own, other)


def relaid_out_proj(w_down):
    n_t = lax.axis_size("tensor")
    chan_local, width = w_down.shape
    blocks = w_down.reshape(chan_local, n_t, width // n_t)
    moved = lax.all_to_all(blocks, "tensor", 1, 0, tiled=True)
    return moved.reshape(n_t * chan_local, width // n_t)


def section_step(x_in, w_in, feat, long_taps, w_out, gain):
    rows = x_in.shape[0]
    chan_local = w_in.shape[1] // 3
    aug = jnp.concatenate([x_in, gain.reshape(1, -1).astype(x_in.dtype)], axis=0)
    full = lax.all_gather(aug, "tensor", axis=1, tiled=True)
    values = full[:rows].astype(jnp.float32)
    gain_all = full[rows].astype(jnp.float32)
    inv_rms = lax.rsqrt(jnp.mean(values * values, axis=1, keepdims=True) + epsilon)
    normed = (values * inv_rms * gain_all[None, :]).astype(jnp.bfloat16)
    projected = jnp.dot(normed, w_in, preferred_element_type=jnp.float32).astype(jnp.bfloat16)
    blocks = lax.axis_size("pipe") * lax.axis_size("seq")
    kv_tail = projected[rows - HALO :, chan_local:]
    q_tail = projected[rows - (KF - 1) :, :chan_local]
    kv_prev, q_prev = lax.ppermute(
        (kv_tail, q_tail), ("pipe", "seq"), [(b, b + 1) for b in range(blocks - 1)]
    )
    q_all = jnp.concatenate([q_prev, projected[:, :chan_local]], axis=0).astype(jnp.float32)
    kv_all = jnp.concatenate([kv_prev, projected[:, chan_local:]], axis=0).astype(jnp.float32)
    q_taps = feat[:, 0, :]
    kv_taps = feat[:, 1:, :].reshape(KF, 2 * chan_local)
    kv_span = KL - 1 + rows
    q_feat = jnp.zeros((rows, chan_local), jnp.float32)
    kv_feat = jnp.zeros((kv_span, 2 * chan_local), jnp.float32)
    for tap_index in range(KF):
        offset = KF - 1 - tap_index
        q_feat = q_feat + q_taps[tap_index] * q_all[offset : offset + rows]
        kv_feat = kv_feat + kv_taps[tap_index] * kv_all[offset : offset + kv_span]
    gated_kv = kv_feat[:, :chan_local] * kv_feat[:, chan_local:]

    def add_tap(tap_index, running):
        shifted = lax.dynamic_slice_in_dim(gated_kv, KL - 1 - tap_index, rows, 0)
        return running + long_taps[tap_index] * shifted

    filtered = lax.fori_loop(0, KL, add_tap, jnp.zeros_like(q_feat))
    y_out = (q_feat * filtered).astype(jnp.bfloat16)
    y_full = lax.all_gather(y_out, "tensor", axis=1, tiled=True)
    mixed = jnp.dot(y_full, w_out, preferred_element_type=jnp.float32)
    return (x_in.astype(jnp.float32) + mixed).astype(jnp.bfloat16)


def local(token_ids, embed_table, in_proj, feat_taps, se_taps, mr_taps, out_proj, norm_gain):
    core = lax.axis_index("pipe")
    w_own = in_proj[0].reshape(in_proj.shape[1], -1)
    feat_own = feat_taps[0]
    gain_own = norm_gain[0]
    wt_own = relaid_out_proj(out_proj[0])
    w_other, feat_other, gain_other, wt_other = swapped((w_own, feat_own, gain_own, wt_own))
    padded_se = jnp.concatenate(
        [se_taps, jnp.zeros((KL - KS, se_taps.shape[1]), jnp.float32)], axis=0
    )
    filters = (padded_se, mr_taps)
    ids = lax.dynamic_index_in_dim(token_ids, core, 0, keepdims=False)
    vocab_ids = jnp.arange(VOCAB, dtype=jnp.int32)
    one_hot = (ids[:, None] == vocab_ids[None, :]).astype(jnp.bfloat16)
    current = jnp.dot(one_hot, embed_table, preferred_element_type=jnp.float32).astype(jnp.bfloat16)
    results = []
    for section in range(2):
        current = section_step(
            current,
            of_section(core, w_own, w_other, section),
            of_section(core, feat_own, feat_other, section),
            filters[section],
            of_section(core, wt_own, wt_other, section),
            of_section(core, gain_own, gain_other, section),
        )
        results.append(current)
    first_mine, second_mine = results
    second_slice_of_first = lax.ppermute(first_mine, "pipe", [(1, 0)])
    first_slice_of_second = lax.ppermute(second_mine, "pipe", [(0, 1)])
    lead = core == 0
    slice_zero = jnp.where(lead, first_mine, first_slice_of_second)
    slice_one = jnp.where(lead, second_slice_of_first, second_mine)
    return jnp.stack([slice_zero, slice_one], axis=0)[None]


def solution(mesh):
    return jax.shard_map(
        local,
        mesh=mesh,
        in_specs=(
            P(None, "seq"),
            P(None, "tensor"),
            P("pipe", None, None, "tensor"),
            P("pipe", None, None, "tensor"),
            P(None, "tensor"),
            P(None, "tensor"),
            P("pipe", "tensor", None),
            P("pipe", "tensor"),
        ),
        out_specs=P("pipe", None, "seq", "tensor"),
        check_vma=False,
    )
```

profile of v0, /device:TPU:1, one launch (start us, length us, event | category | flops | bytes accessed | tf_op | source)
XLA Modules:
  0.0 497.7 jit_solution(15193292453883227668)
XLA Ops:
  7.3 3.3 collective-permute-start.1
  12.3 8.9 %copy.10 = bf16[1,8192,3,128]{1,3,2,0:T(8,128)(2,1)} copy(bf16[1,8192,3,128]{3,1,2,0:T(8,128)(2,1)} %param.14) | data formatting | bytes 12582912 | tf_op args[2]
  24.1 9.5 %all-to-all-start = ((bf16[128,32,256]{0,2,1:T(8,128)(2,1)}), bf16[128,32,256]{0,2,1:T(8,128)(2,1)S(1)}, u32[]{:S(2)}, u32[]{:S(2)}) async-start(bf16[128,32,256]{0,2,1:T(8,128)(2,1)} %bitcast.58), calls=%async_computation | async-start | bytes 4194304 | tf_op jit(solution)/shard_map/all_to_all | solution.py:26
  33.7 75.9 %all-gather.5.cloned.1.call-done = bf16[193,8192]{1,0:T(8,128)(2,1)} async-done(((bf16[193,256]{1,0:T(8,128)(2,1)}), bf16[193,8192]{1,0:T(8,128)(2,1)}) %all-gather.5.cloned.1.call-update) | async-done | bytes 3162128 | tf_op jit(solution)/shard_map/all_gather | solution.py:34
  109.6 2.6 fusion
  113.1 6.0 %fusion.26 = bf16[192,384]{1,0:T(8,128)(2,1)S(1)} fusion(bf16[8192,384]{0,1:T(8,128)(2,1)} %bitcast.60, bf16[8192,384]{0,1:T(8,128)(2,1)} %collective-permute-done.2, pred[]{:T(512)S(6)} %eq.12, f32[8192]{0:T(1024)S(1)} %bitcast.65, f32[192]{0:T(256)S(1)} %add_rsqrt_fusion.1, bf16[193,8192]{1,0:T(8,128)(2,1)} %all-gather.5.cloned.1.call-done), kind=kOutput, calls=%fused_computation.32 | convolution fusion | flops 1217470464 | bytes 15909633 | tf_op jit(solution)/shard_map/dot_general | solution.py:39
  119.1 3.1 collective-permute-start.3
  122.3 3.0 collective-permute-start.4
  125.3 2.7 collective-permute-done.3
  128.1 2.7 collective-permute-done.4
  131.0 10.6 %while.32 = (s32[]{:T(128)}, f32[192,128]{1,0:T(8,128)S(1)}, f32[128,128]{1,0:T(8,128)S(1)}, f32[319,128]{1,0:T(8,128)S(1)}, s32[]{:T(128)}, /*index=5*/s32[]{:T(128)}, s32[]{:T(128)}, s32[]{:T(128)}) while((s32[]{:T(128)}, f32[192,128]{1,0:T(8,128)S(1)}, f32[128,128]{1,0:T(8,128)S(1)}, f32[319,128]{1,0:T(8,128)S(1)}, s32[]{:T(128)}, ...), condition=%wide.region_2.3_spmd.clone, body=%wide.region_1.2_spmd.clone.sunk | while | flops 73735 | bytes 296597 | solution.py:63
  142.4 2.9 copy.12
  145.8 4.0 collective-permute-done.5
  149.8 60.7 %all-gather.7.cloned.1.call-done = bf16[192,4096]{1,0:T(8,128)(2,1)} async-done(((bf16[192,128]{1,0:T(8,128)(2,1)}), bf16[192,4096]{1,0:T(8,128)(2,1)}) %all-gather.7.cloned.1.call-update) | async-done | bytes 1572880 | tf_op jit(solution)/shard_map/all_gather | solution.py:65
  213.3 80.0 %all-gather.9.cloned.1.call-done = bf16[193,8192]{1,0:T(8,128)(2,1)} async-done(((bf16[193,256]{1,0:T(8,128)(2,1)}), bf16[193,8192]{1,0:T(8,128)(2,1)}) %all-gather.9.cloned.1.call-update) | async-done | bytes 3162128 | tf_op jit(solution)/shard_map/all_gather | solution.py:34
  293.3 2.6 fusion.3
  296.8 6.0 %fusion.31 = bf16[192,384]{1,0:T(8,128)(2,1)S(1)} fusion(bf16[8192,384]{0,1:T(8,128)(2,1)} %bitcast.61, bf16[8192,384]{0,1:T(8,128)(2,1)} %collective-permute-done.2, pred[]{:T(512)S(6)} %eq.33, f32[8192]{0:T(1024)S(1)} %bitcast.66, f32[192]{0:T(256)S(1)} %add_rsqrt_fusion, bf16[193,8192]{1,0:T(8,128)(2,1)} %all-gather.9.cloned.1.call-done), kind=kOutput, calls=%fused_computation.33 | convolution fusion | flops 1217470464 | bytes 15909633 | tf_op jit(solution)/shard_map/dot_general | solution.py:39
  302.8 3.2 collective-permute-start.6
  306.1 3.1 collective-permute-start.7
  311.5 2.7 collective-permute-done.7
  314.4 96.0 %while.33 = (s32[]{:T(128)}, f32[192,128]{1,0:T(8,128)S(1)}, f32[128,128]{1,0:T(8,128)}, f32[319,128]{1,0:T(8,128)S(1)}, s32[]{:T(128)}, /*index=5*/s32[]{:T(128)}, s32[]{:T(128)}, s32[]{:T(128)}) while((s32[]{:T(128)}, f32[192,128]{1,0:T(8,128)S(1)}, f32[128,128]{1,0:T(8,128)}, f32[319,128]{1,0:T(8,128)S(1)}, s32[]{:T(128)}, ...), condition=%wide.region_5.6_spmd.clone, body=%wide.region_4.5_spmd.clone.sunk | while | flops 73735 | bytes 296597 | solution.py:63
  411.1 2.5 collective-permute-start.9
  413.6 68.0 %all-gather.11.cloned.1.call-done = bf16[192,4096]{1,0:T(8,128)(2,1)} async-done(((bf16[192,128]{1,0:T(8,128)(2,1)}), bf16[192,4096]{1,0:T(8,128)(2,1)}) %all-gather.11.cloned.1.call-update) | async-done | bytes 1572880 | tf_op jit(solution)/shard_map/all_gather | solution.py:65
  485.0 5.4 %collective-permute-done.8 = bf16[192,256]{1,0:T(8,128)(2,1)S(1)} collective-permute-done((bf16[192,256]{1,0:T(8,128)(2,1)S(1)}, bf16[192,256]{1,0:T(8,128)(2,1)S(1)}, u32[]{:S(2)}, u32[]{:S(2)}) %collective-permute-start.8) | collective-permute-done | bytes 98336 | tf_op jit(solution)/shard_map/ppermute | solution.py:98
  (587 shorter events, 117.1 us)
Async XLA Ops:
  6.5 4.7 copy-start
  6.5 103.0 %all-gather.5.cloned.1.call-start = ((), (), s32[]{:S(2)}) async-start(), calls=%async_computation.1 | async-start | bytes 3379200 | tf_op jit(solution)/shard_map/all_gather | solution.py:34
  7.3 4.3 collective-permute-start.1
  12.3 9.0 %copy-start.3 = (f32[1,3,3,128]{3,0,2,1:T(1,128)S(1)}, f32[1,3,3,128]{3,0,2,1:T(1,128)}, u32[]{:S(2)}) copy-start(f32[1,3,3,128]{3,0,2,1:T(1,128)} %param.15) | copy-start | bytes 13828
  12.3 9.4 %copy-start.1 = (bf16[1,128,8192]{2,1,0:T(8,128)(2,1)S(1)}, bf16[1,128,8192]{2,1,0:T(8,128)(2,1)}, u32[]{:S(2)}) copy-start(bf16[1,128,8192]{2,1,0:T(8,128)(2,1)} %param.18) | copy-start | bytes 6291460
  21.1 92.0 %collective-permute-start.2 = (bf16[8192,384]{0,1:T(8,128)(2,1)}, bf16[8192,384]{0,1:T(8,128)(2,1)}, u32[]{:S(2)}, u32[]{:S(2)}) collective-permute-start(bf16[8192,384]{0,1:T(8,128)(2,1)} %bitcast.59), channel_id=1, source_target_pairs={{0,128},{128,0},{1,129},{129,1},{2,130},{130,2},{3,131},{131,3},{4... | collective-permute-start | bytes 18874376 | tf_op jit(solution)/shard_map/ppermute | solution.py:15
  21.3 12.4 %copy-start.4 = (f32[7,128]{1,0:T(8,128)S(1)}, f32[7,128]{1,0:T(8,128)}, u32[]{:S(2)}) copy-start(f32[7,128]{1,0:T(8,128)} %param.16) | copy-start | bytes 10756
  21.3 12.4 %collective-permute-start = (f32[3,3,128]{2,1,0:T(4,128)S(1)}, f32[3,3,128]{2,1,0:T(4,128)S(1)}, u32[]{:S(2)}, u32[]{:S(2)}) collective-permute-start(f32[3,3,128]{2,1,0:T(4,128)S(1)} %bitcast.67), channel_id=1, source_target_pairs={{0,128},{128,0},{1,129},{129,1},{2,130},{130,2},{3,131},{131,3},{4... | collective-permute-start | bytes 13832 | tf_op jit(solution)/shard_map/ppermute | solution.py:15
  24.1 118.2 %all-to-all-start = ((bf16[128,32,256]{0,2,1:T(8,128)(2,1)}), bf16[128,32,256]{0,2,1:T(8,128)(2,1)S(1)}, u32[]{:S(2)}, u32[]{:S(2)}) async-start(bf16[128,32,256]{0,2,1:T(8,128)(2,1)} %bitcast.58), calls=%async_computation | async-start | bytes 4194304 | tf_op jit(solution)/shard_map/all_to_all | solution.py:26
  33.6 176.9 %all-gather.7.cloned.1.call-start = ((), (), s32[]{:S(2)}) async-start(), calls=%async_computation.2 | async-start | bytes 1622016 | tf_op jit(solution)/shard_map/all_gather | solution.py:65
  119.1 8.9 %collective-permute-start.3 = (bf16[2,128]{1,0:T(2,128)(2,1)S(1)}, bf16[2,128]{1,0:T(2,128)(2,1)S(1)}, u32[]{:S(2)}, u32[]{:S(2)}) collective-permute-start(bf16[2,128]{1,0:T(2,128)(2,1)S(1)} %slice.191), channel_id=1, source_target_pairs={{0,32},{32,64},{64,96},{96,128},{128,160},{160,192},{192,224},{1,3... | collective-permute-start | bytes 1544 | tf_op jit(solution)/shard_map/ppermute | solution.py:43
  122.3 8.5 %collective-permute-start.4 = (bf16[129,256]{1,0:T(8,128)(2,1)S(1)}, bf16[129,256]{1,0:T(8,128)(2,1)S(1)}, u32[]{:S(2)}, u32[]{:S(2)}) collective-permute-start(bf16[129,256]{1,0:T(8,128)(2,1)S(1)} %slice.199), channel_id=1, source_target_pairs={{0,32},{32,64},{64,96},{96,128},{128,160},{160,192},{192,224},{1,3... | collective-permute-start | bytes 198152 | tf_op jit(solution)/shard_map/ppermute | solution.py:43
  142.3 151.0 %all-gather.9.cloned.1.call-start = ((), (), s32[]{:S(2)}) async-start(), calls=%async_computation.3 | async-start | bytes 3379200 | tf_op jit(solution)/shard_map/all_gather | solution.py:34
  145.3 4.5 collective-permute-start.5
  149.8 62.7 %copy-start.5 = (bf16[4096,256]{1,0:T(8,128)(2,1)}, bf16[4096,256]{1,0:T(8,128)(2,1)S(1)}, u32[]{:S(2)}) copy-start(bf16[4096,256]{1,0:T(8,128)(2,1)S(1)} %collective-permute-done.5) | copy-start | bytes 6291460
  213.2 268.4 %all-gather.11.cloned.1.call-start = ((), (), s32[]{:S(2)}) async-start(), calls=%async_computation.4 | async-start | bytes 1622016 | tf_op jit(solution)/shard_map/all_gather | solution.py:65
  302.8 178.8 %copy-start.2 = (bf16[32,128,1,256]{3,1,0,2:T(8,128)(2,1)S(1)}, bf16[32,128,1,256]{3,1,0,2:T(8,128)(2,1)}, u32[]{:S(2)}) copy-start(bf16[32,128,1,256]{3,1,0,2:T(8,128)(2,1)} %copy.12) | copy-start | bytes 6291460
  302.8 8.6 %collective-permute-start.6 = (bf16[2,128]{1,0:T(2,128)(2,1)S(1)}, bf16[2,128]{1,0:T(2,128)(2,1)S(1)}, u32[]{:S(2)}, u32[]{:S(2)}) collective-permute-start(bf16[2,128]{1,0:T(2,128)(2,1)S(1)} %slice.211), channel_id=1, source_target_pairs={{0,32},{32,64},{64,96},{96,128},{128,160},{160,192},{192,224},{1,3... | collective-permute-start | bytes 1544 | tf_op jit(solution)/shard_map/ppermute | solution.py:43
  306.1 8.1 %collective-permute-start.7 = (bf16[129,256]{1,0:T(8,128)(2,1)S(1)}, bf16[129,256]{1,0:T(8,128)(2,1)S(1)}, u32[]{:S(2)}, u32[]{:S(2)}) collective-permute-start(bf16[129,256]{1,0:T(8,128)(2,1)S(1)} %slice.219), channel_id=1, source_target_pairs={{0,32},{32,64},{64,96},{96,128},{128,160},{160,192},{192,224},{1,3... | collective-permute-start | bytes 198152 | tf_op jit(solution)/shard_map/ppermute | solution.py:43
  411.1 72.6 %collective-permute-start.9 = (bf16[192,256]{1,0:T(8,128)(2,1)S(1)}, bf16[192,256]{1,0:T(8,128)(2,1)S(1)}, u32[]{:S(2)}, u32[]{:S(2)}) collective-permute-start(bf16[192,256]{1,0:T(8,128)(2,1)S(1)} %fusion.39), channel_id=1, source_target_pairs={{128,0},{129,1},{130,2},{131,3},{132,4},{133,5},{134,6},{135,7},{1... | collective-permute-start | bytes 294920 | tf_op jit(solution)/shard_map/ppermute | solution.py:97
  483.7 6.7 %collective-permute-start.8 = (bf16[192,256]{1,0:T(8,128)(2,1)S(1)}, bf16[192,256]{1,0:T(8,128)(2,1)S(1)}, u32[]{:S(2)}, u32[]{:S(2)}) collective-permute-start(bf16[192,256]{1,0:T(8,128)(2,1)S(1)} %get-tuple-element.274), channel_id=1, source_target_pairs={{0,128},{1,129},{2,130},{3,131},{4,132},{5,133},{6,134},{7,135},{8... | collective-permute-start | bytes 294920 | tf_op jit(solution)/shard_map/ppermute | solution.py:98
Sparse Core Ops, SparseCore 0:
  12.4 97.1 all-gather.4
  142.4 68.0 all-gather.6
  213.3 79.9 all-gather.8
  411.2 70.3 all-gather.10
where the time goes:
time: 502 us; the launch traced here: 498 us
  waiting for transfers between devices  305 us (61%)
  local copies, waits for them, and re-layouts  105 us (21%)
  starting transfers between devices  30.1 us (6%)
  other arithmetic  19.8 us (4%)
  matrix products  16.2 us (3%)
  between operations  13.5 us (3%)
  loops' own time  8.15 us (2%)
    all_gather x2, waiting for transfers between devices, section_step(): full = lax.all_gather(aug, 'tensor', axis=1, tiled=True)  156 us
    all_gather x2, waiting for transfers between devices, section_step(): y_full = lax.all_gather(y_out, 'tensor', axis=1, tiled=True)  129 us
    mul x256, local copies, waits for them, and re-layouts, add_tap(): return running + long_taps[tap_index] * shifted  90.3 us
    ppermute x4, starting transfers between devices, section_step(): lax.ppermute((kv_tail, q_tail), ('pipe', 'seq'), [(b, b + 1) for b in ran...  12.4 us
    dot_general x2, matrix products, section_step(): jnp.dot(normed, w_in, preferred_element_type=jnp.float32)  12 us
    unnamed x15, local copies, waits for them, and re-layouts  11.3 us
    ppermute x4, waiting for transfers between devices, section_step(): lax.ppermute((kv_tail, q_tail), ('pipe', 'seq'), [(b, b + 1) for b in ran...  10.5 us
  transfers between devices with their start and end apart: 15, of which 10 were waited for; matrix products, arithmetic and copies ran while one was open for 7% of the time, Pallas kernels for 0%

commit v1 on v0

--- a/solution.py
+++ b/solution.py
@@ -62,7 +62,8 @@
 
     filtered = lax.fori_loop(0, KL, add_tap, jnp.zeros_like(q_feat))
     y_out = (q_feat * filtered).astype(jnp.bfloat16)
-    y_full = lax.all_gather(y_out, "tensor", axis=1, tiled=True)
+    copies = jnp.concatenate([y_out] * lax.axis_size("tensor"), axis=1)
+    y_full = lax.all_to_all(copies, "tensor", 1, 1, tiled=True)
     mixed = jnp.dot(y_full, w_out, preferred_element_type=jnp.float32)
     return (x_in.astype(jnp.float32) + mixed).astype(jnp.bfloat16)
 

time: 502 us -> 450 us (0.90)
  waiting for transfers between devices: 305 us -> 233 us
  starting transfers between devices: 30.1 us -> 46 us
    all_gather x2 -> x0, waiting for transfers between devices: 129 us -> none  [section_step(): y_full = lax.all_gather(y_out, 'tensor', axis=1, tiled=True)]
    all_to_all x0 -> x2, waiting for transfers between devices: none -> 65.1 us  [section_step(): y_full = lax.all_to_all(copies, 'tensor', 1, 1, tiled=True)]
    all_to_all x0 -> x2, starting transfers between devices: none -> 15.3 us  [section_step(): y_full = lax.all_to_all(copies, 'tensor', 1, 1, tiled=True)]
    all_gather x2, waiting for transfers between devices: 156 us -> 149 us  [section_step(): full = lax.all_gather(aug, 'tensor', axis=1, tiled=True)]
    unnamed x15 -> x75, local copies, waits for them, and re-layouts: 11.3 us -> 12.3 us
  transfers between devices with their start and end apart: 15 -> 15, of which waited for: 10 -> 10; matrix products, arithmetic and copies ran while one was open for 7% -> 8% of each run, Pallas kernels for 0% -> 0%
where the time goes in v1:
time: 450 us; the launch traced here: 445 us
  waiting for transfers between devices  233 us (52%)
  local copies, waits for them, and re-layouts  110 us (24%)
  starting transfers between devices  46 us (10%)
  other arithmetic  18.5 us (4%)
  matrix products  16.2 us (4%)
  between operations  14.2 us (3%)
  loops' own time  8.15 us (2%)
    all_gather x2, waiting for transfers between devices, section_step(): full = lax.all_gather(aug, 'tensor', axis=1, tiled=True)  149 us
    mul x256, local copies, waits for them, and re-layouts, add_tap(): return running + long_taps[tap_index] * shifted  90.3 us
    all_to_all x2, waiting for transfers between devices, section_step(): y_full = lax.all_to_all(copies, 'tensor', 1, 1, tiled=True)  65.1 us
    all_to_all x2, starting transfers between devices, section_step(): y_full = lax.all_to_all(copies, 'tensor', 1, 1, tiled=True)  15.3 us
    ppermute x4, starting transfers between devices, section_step(): lax.ppermute((kv_tail, q_tail), ('pipe', 'seq'), [(b, b + 1) for b in ran...  12.5 us
    unnamed x75, local copies, waits for them, and re-layouts  12.3 us
    dot_general x2, matrix products, section_step(): jnp.dot(normed, w_in, preferred_element_type=jnp.float32)  12 us
    ppermute x4, waiting for transfers between devices, section_step(): lax.ppermute((kv_tail, q_tail), ('pipe', 'seq'), [(b, b + 1) for b in ran...  10.4 us
  transfers between devices with their start and end apart: 15, of which 10 were waited for; matrix products, arithmetic and copies ran while one was open for 8% of the time, Pallas kernels for 0%

profile of v1, /device:TPU:1, one launch (start us, length us, event | category | flops | bytes accessed | tf_op | source)
XLA Modules:
  0.0 445.3 jit_solution(16418198322817154175)
XLA Ops:
  7.3 3.3 collective-permute-start.1
  12.3 8.9 %copy.18 = bf16[1,8192,3,128]{1,3,2,0:T(8,128)(2,1)} copy(bf16[1,8192,3,128]{3,1,2,0:T(8,128)(2,1)} %param.14) | data formatting | bytes 12582912 | tf_op args[2]
  24.1 9.6 %all-to-all-start.1 = ((bf16[128,32,256]{0,2,1:T(8,128)(2,1)}), bf16[128,32,256]{0,2,1:T(8,128)(2,1)S(1)}, u32[]{:S(2)}, u32[]{:S(2)}) async-start(bf16[128,32,256]{0,2,1:T(8,128)(2,1)} %bitcast.84), calls=%async_computation.1 | async-start | bytes 4194304 | tf_op jit(solution)/shard_map/all_to_all | solution.py:26
  33.8 75.6 %all-gather.3.cloned.1.call-done = bf16[193,8192]{1,0:T(8,128)(2,1)} async-done(((bf16[193,256]{1,0:T(8,128)(2,1)}), bf16[193,8192]{1,0:T(8,128)(2,1)}) %all-gather.3.cloned.1.call-update) | async-done | bytes 3162128 | tf_op jit(solution)/shard_map/all_gather | solution.py:34
  112.9 6.0 %fusion.30 = bf16[192,384]{1,0:T(8,128)(2,1)S(1)} fusion(bf16[8192,384]{0,1:T(8,128)(2,1)} %bitcast.86, bf16[8192,384]{0,1:T(8,128)(2,1)} %collective-permute-done.2, pred[]{:T(512)S(6)} %eq.12, f32[8192]{0:T(1024)S(1)} %bitcast.91, f32[192]{0:T(256)S(1)} %add_rsqrt_fusion.1, bf16[193,8192]{1,0:T(8,128)(2,1)} %all-gather.3.cloned.1.call-done), kind=kOutput, calls=%fused_computation.38 | convolution fusion | flops 1217470464 | bytes 15909633 | tf_op jit(solution)/shard_map/dot_general | solution.py:39
  118.9 3.1 collective-permute-start.3
  122.1 3.2 collective-permute-start.4
  125.3 2.7 collective-permute-done.3
  128.1 2.7 collective-permute-done.4
  131.0 10.6 %while.32 = (s32[]{:T(128)}, f32[192,128]{1,0:T(8,128)S(1)}, f32[128,128]{1,0:T(8,128)S(1)}, f32[319,128]{1,0:T(8,128)S(1)}, s32[]{:T(128)}, /*index=5*/s32[]{:T(128)}, s32[]{:T(128)}, s32[]{:T(128)}) while((s32[]{:T(128)}, f32[192,128]{1,0:T(8,128)S(1)}, f32[128,128]{1,0:T(8,128)S(1)}, f32[319,128]{1,0:T(8,128)S(1)}, s32[]{:T(128)}, ...), condition=%wide.region_2.3_spmd.clone, body=%wide.region_1.2_spmd.clone.sunk | while | flops 73735 | bytes 296597 | solution.py:63
  144.0 6.3 %all-to-all-start = ((bf16[192,32,128]{2,0,1:T(8,128)(2,1)}), bf16[192,32,128]{2,0,1:T(8,128)(2,1)}, u32[]{:S(2)}, u32[]{:S(2)}) async-start(bf16[192,32,128]{2,0,1:T(8,128)(2,1)} %copy_bitcast_fusion.1), calls=%async_computation | async-start | bytes 3145728 | tf_op jit(solution)/shard_map/all_to_all | solution.py:66
  150.3 2.9 copy.22
  153.9 4.0 collective-permute-done.5
  157.9 30.1 %all-to-all-done = bf16[192,32,128]{2,0,1:T(8,128)(2,1)} async-done(((bf16[192,32,128]{2,0,1:T(8,128)(2,1)}), bf16[192,32,128]{2,0,1:T(8,128)(2,1)}, u32[]{:S(2)}, u32[]{:S(2)}) %all-to-all-start) | async-done | bytes 1572896 | tf_op jit(solution)/shard_map/all_to_all | solution.py:66
  190.7 73.9 %all-gather.5.cloned.1.call-done = bf16[193,8192]{1,0:T(8,128)(2,1)} async-done(((bf16[193,256]{1,0:T(8,128)(2,1)}), bf16[193,8192]{1,0:T(8,128)(2,1)}) %all-gather.5.cloned.1.call-update) | async-done | bytes 3162128 | tf_op jit(solution)/shard_map/all_gather | solution.py:34
  268.1 6.0 %fusion.35 = bf16[192,384]{1,0:T(8,128)(2,1)S(1)} fusion(bf16[8192,384]{0,1:T(8,128)(2,1)} %bitcast.87, bf16[8192,384]{0,1:T(8,128)(2,1)} %collective-permute-done.2, pred[]{:T(512)S(6)} %eq.33, f32[8192]{0:T(1024)S(1)} %bitcast.92, f32[192]{0:T(256)S(1)} %add_rsqrt_fusion, bf16[193,8192]{1,0:T(8,128)(2,1)} %all-gather.5.cloned.1.call-done), kind=kOutput, calls=%fused_computation.39 | convolution fusion | flops 1217470464 | bytes 15909633 | tf_op jit(solution)/shard_map/dot_general | solution.py:39
  274.1 3.1 collective-permute-start.6
  277.3 3.1 collective-permute-start.7
  282.7 2.7 collective-permute-done.7
  285.6 96.0 %while.33 = (s32[]{:T(128)}, f32[192,128]{1,0:T(8,128)S(1)}, f32[128,128]{1,0:T(8,128)}, f32[319,128]{1,0:T(8,128)S(1)}, s32[]{:T(128)}, /*index=5*/s32[]{:T(128)}, s32[]{:T(128)}, s32[]{:T(128)}) while((s32[]{:T(128)}, f32[192,128]{1,0:T(8,128)S(1)}, f32[128,128]{1,0:T(8,128)}, f32[319,128]{1,0:T(8,128)S(1)}, s32[]{:T(128)}, ...), condition=%wide.region_5.6_spmd.clone, body=%wide.region_4.5_spmd.clone.sunk | while | flops 73735 | bytes 296597 | solution.py:63
  383.9 9.0 %all-to-all-start.2 = ((bf16[192,32,128]{2,0,1:T(8,128)(2,1)}), bf16[192,32,128]{2,0,1:T(8,128)(2,1)}, u32[]{:S(2)}, u32[]{:S(2)}) async-start(bf16[192,32,128]{2,0,1:T(8,128)(2,1)} %copy_bitcast_fusion), calls=%async_computation.2 | async-start | bytes 3145728 | tf_op jit(solution)/shard_map/all_to_all | solution.py:66
  392.9 2.8 collective-permute-start.9
  395.7 35.0 %all-to-all-done.2 = bf16[192,32,128]{2,0,1:T(8,128)(2,1)} async-done(((bf16[192,32,128]{2,0,1:T(8,128)(2,1)}), bf16[192,32,128]{2,0,1:T(8,128)(2,1)}, u32[]{:S(2)}, u32[]{:S(2)}) %all-to-all-start.2) | async-done | bytes 1572896 | tf_op jit(solution)/shard_map/all_to_all | solution.py:66
  434.0 3.8 collective-permute-done.8
  (649 shorter events, 125.3 us)
Async XLA Ops:
  6.5 4.7 %copy-start = (bf16[512,256]{1,0:T(8,128)(2,1)S(1)}, bf16[512,256]{1,0:T(8,128)(2,1)}, u32[]{:S(2)}) copy-start(bf16[512,256]{1,0:T(8,128)(2,1)} %param.13) | copy-start | bytes 786436
  6.5 102.8 %all-gather.3.cloned.1.call-start = ((), (), s32[]{:S(2)}) async-start(), calls=%async_computation.3 | async-start | bytes 3379200 | tf_op jit(solution)/shard_map/all_gather | solution.py:34
  7.3 4.3 collective-permute-start.1
  12.3 9.0 %copy-start.3 = (f32[1,3,3,128]{3,0,2,1:T(1,128)S(1)}, f32[1,3,3,128]{3,0,2,1:T(1,128)}, u32[]{:S(2)}) copy-start(f32[1,3,3,128]{3,0,2,1:T(1,128)} %param.15) | copy-start | bytes 13828
  12.3 9.4 %copy-start.1 = (bf16[1,128,8192]{2,1,0:T(8,128)(2,1)S(1)}, bf16[1,128,8192]{2,1,0:T(8,128)(2,1)}, u32[]{:S(2)}) copy-start(bf16[1,128,8192]{2,1,0:T(8,128)(2,1)} %param.18) | copy-start | bytes 6291460
  21.1 91.8 %collective-permute-start.2 = (bf16[8192,384]{0,1:T(8,128)(2,1)}, bf16[8192,384]{0,1:T(8,128)(2,1)}, u32[]{:S(2)}, u32[]{:S(2)}) collective-permute-start(bf16[8192,384]{0,1:T(8,128)(2,1)} %bitcast.85), channel_id=1, source_target_pairs={{0,128},{128,0},{1,129},{129,1},{2,130},{130,2},{3,131},{131,3},{4... | collective-permute-start | bytes 18874376 | tf_op jit(solution)/shard_map/ppermute | solution.py:15
  21.3 12.5 %collective-permute-start = (f32[3,3,128]{2,1,0:T(4,128)S(1)}, f32[3,3,128]{2,1,0:T(4,128)S(1)}, u32[]{:S(2)}, u32[]{:S(2)}) collective-permute-start(f32[3,3,128]{2,1,0:T(4,128)S(1)} %bitcast.93), channel_id=1, source_target_pairs={{0,128},{128,0},{1,129},{129,1},{2,130},{130,2},{3,131},{131,3},{4... | collective-permute-start | bytes 13832 | tf_op jit(solution)/shard_map/ppermute | solution.py:15
  24.1 9.6 %copy-start.4 = (f32[7,128]{1,0:T(8,128)S(1)}, f32[7,128]{1,0:T(8,128)}, u32[]{:S(2)}) copy-start(f32[7,128]{1,0:T(8,128)} %param.16) | copy-start | bytes 10756
  24.1 119.9 %all-to-all-start.1 = ((bf16[128,32,256]{0,2,1:T(8,128)(2,1)}), bf16[128,32,256]{0,2,1:T(8,128)(2,1)S(1)}, u32[]{:S(2)}, u32[]{:S(2)}) async-start(bf16[128,32,256]{0,2,1:T(8,128)(2,1)} %bitcast.84), calls=%async_computation.1 | async-start | bytes 4194304 | tf_op jit(solution)/shard_map/all_to_all | solution.py:26
  118.9 9.1 %collective-permute-start.3 = (bf16[2,128]{1,0:T(2,128)(2,1)S(1)}, bf16[2,128]{1,0:T(2,128)(2,1)S(1)}, u32[]{:S(2)}, u32[]{:S(2)}) collective-permute-start(bf16[2,128]{1,0:T(2,128)(2,1)S(1)} %slice.191), channel_id=1, source_target_pairs={{0,32},{32,64},{64,96},{96,128},{128,160},{160,192},{192,224},{1,3... | collective-permute-start | bytes 1544 | tf_op jit(solution)/shard_map/ppermute | solution.py:43
  122.1 8.7 %collective-permute-start.4 = (bf16[129,256]{1,0:T(8,128)(2,1)S(1)}, bf16[129,256]{1,0:T(8,128)(2,1)S(1)}, u32[]{:S(2)}, u32[]{:S(2)}) collective-permute-start(bf16[129,256]{1,0:T(8,128)(2,1)S(1)} %slice.199), channel_id=1, source_target_pairs={{0,32},{32,64},{64,96},{96,128},{128,160},{160,192},{192,224},{1,3... | collective-permute-start | bytes 198152 | tf_op jit(solution)/shard_map/ppermute | solution.py:43
  144.0 44.1 %all-to-all-start = ((bf16[192,32,128]{2,0,1:T(8,128)(2,1)}), bf16[192,32,128]{2,0,1:T(8,128)(2,1)}, u32[]{:S(2)}, u32[]{:S(2)}) async-start(bf16[192,32,128]{2,0,1:T(8,128)(2,1)} %copy_bitcast_fusion.1), calls=%async_computation | async-start | bytes 3145728 | tf_op jit(solution)/shard_map/all_to_all | solution.py:66
  150.3 114.3 %all-gather.5.cloned.1.call-start = ((), (), s32[]{:S(2)}) async-start(), calls=%async_computation.4 | async-start | bytes 3379200 | tf_op jit(solution)/shard_map/all_gather | solution.py:34
  153.3 4.7 %collective-permute-start.5 = (bf16[4096,256]{1,0:T(8,128)(2,1)}, bf16[4096,256]{1,0:T(8,128)(2,1)S(1)}, u32[]{:S(2)}, u32[]{:S(2)}) collective-permute-start(bf16[4096,256]{1,0:T(8,128)(2,1)} %bitcast.88), channel_id=1, source_target_pairs={{0,128},{128,0},{1,129},{129,1},{2,130},{130,2},{3,131},{131,3},{4... | collective-permute-start | bytes 6291464 | tf_op jit(solution)/shard_map/ppermute | solution.py:15
  157.9 32.1 %copy-start.5 = (bf16[4096,256]{1,0:T(8,128)(2,1)}, bf16[4096,256]{1,0:T(8,128)(2,1)S(1)}, u32[]{:S(2)}) copy-start(bf16[4096,256]{1,0:T(8,128)(2,1)S(1)} %collective-permute-done.5) | copy-start | bytes 6291460
  274.1 8.5 %collective-permute-start.6 = (bf16[2,128]{1,0:T(2,128)(2,1)S(1)}, bf16[2,128]{1,0:T(2,128)(2,1)S(1)}, u32[]{:S(2)}, u32[]{:S(2)}) collective-permute-start(bf16[2,128]{1,0:T(2,128)(2,1)S(1)} %slice.211), channel_id=1, source_target_pairs={{0,32},{32,64},{64,96},{96,128},{128,160},{160,192},{192,224},{1,3... | collective-permute-start | bytes 1544 | tf_op jit(solution)/shard_map/ppermute | solution.py:43
  277.3 8.1 %collective-permute-start.7 = (bf16[129,256]{1,0:T(8,128)(2,1)S(1)}, bf16[129,256]{1,0:T(8,128)(2,1)S(1)}, u32[]{:S(2)}, u32[]{:S(2)}) collective-permute-start(bf16[129,256]{1,0:T(8,128)(2,1)S(1)} %slice.219), channel_id=1, source_target_pairs={{0,32},{32,64},{64,96},{96,128},{128,160},{160,192},{192,224},{1,3... | collective-permute-start | bytes 198152 | tf_op jit(solution)/shard_map/ppermute | solution.py:43
  383.9 46.7 %copy-start.2 = (bf16[32,128,1,256]{3,1,0,2:T(8,128)(2,1)S(1)}, bf16[32,128,1,256]{3,1,0,2:T(8,128)(2,1)}, u32[]{:S(2)}) copy-start(bf16[32,128,1,256]{3,1,0,2:T(8,128)(2,1)} %copy.22) | copy-start | bytes 6291460
  383.9 46.7 %all-to-all-start.2 = ((bf16[192,32,128]{2,0,1:T(8,128)(2,1)}), bf16[192,32,128]{2,0,1:T(8,128)(2,1)}, u32[]{:S(2)}, u32[]{:S(2)}) async-start(bf16[192,32,128]{2,0,1:T(8,128)(2,1)} %copy_bitcast_fusion), calls=%async_computation.2 | async-start | bytes 3145728 | tf_op jit(solution)/shard_map/all_to_all | solution.py:66
  392.9 39.7 %collective-permute-start.9 = (bf16[192,256]{1,0:T(8,128)(2,1)S(1)}, bf16[192,256]{1,0:T(8,128)(2,1)S(1)}, u32[]{:S(2)}, u32[]{:S(2)}) collective-permute-start(bf16[192,256]{1,0:T(8,128)(2,1)S(1)} %fusion.45), channel_id=1, source_target_pairs={{128,0},{129,1},{130,2},{131,3},{132,4},{133,5},{134,6},{135,7},{1... | collective-permute-start | bytes 294920 | tf_op jit(solution)/shard_map/ppermute | solution.py:98
  432.7 5.1 %collective-permute-start.8 = (bf16[192,256]{1,0:T(8,128)(2,1)S(1)}, bf16[192,256]{1,0:T(8,128)(2,1)S(1)}, u32[]{:S(2)}, u32[]{:S(2)}) collective-permute-start(bf16[192,256]{1,0:T(8,128)(2,1)S(1)} %get-tuple-element.274), channel_id=1, source_target_pairs={{0,128},{1,129},{2,130},{3,131},{4,132},{5,133},{6,134},{7,135},{8... | collective-permute-start | bytes 294920 | tf_op jit(solution)/shard_map/ppermute | solution.py:99
Sparse Core Ops, SparseCore 0:
  12.4 96.9 all-gather.2
  190.8 73.7 all-gather.4
